TPU v7x, 128 devices: a whole 4x4x4 slice. The times are simulated.
128 devices in a mesh: owner: 32 (over z, x, core), tensor: 4 (over y).
Axes of the slice: x: 4, y: 4, z: 4, core: 2. Of those that a mesh axis runs over, the one named last changes fastest.
Arguments:
- gradients: bfloat16 [160, 1536, 512], P(None, 'owner', 'tensor'), may hold values from -12 to 12
- moments: bfloat16 [160, 1536, 512], P(None, 'owner', 'tensor'), may hold values from -12 to 12
- stats: float32 [256, 512, 512], P(('owner', 'tensor')), may hold values from -1 to 11, as said below
- bases: float32 [256, 512, 512], P(('owner', 'tensor')), may hold values from -1 to 2
- second: bfloat16 [256, 1536, 512], P(('owner', 'tensor')), may hold values from 0.19921875 to 8
- owner_list: int32 [160], replicated, may hold values from 0 to 127, as said below
Outputs:
- new_moments: bfloat16 [160, 1536, 512], P(None, 'owner', 'tensor')
- update: bfloat16 [160, 1536, 512], P(None, 'owner', 'tensor')
- new_stats: float32 [256, 512, 512], P(('owner', 'tensor'))
- new_bases: float32 [256, 512, 512], P(('owner', 'tensor'))
- new_second: bfloat16 [256, 1536, 512], P(('owner', 'tensor'))
Inputs may be any that keep to these rules, and one draw needn't show every extreme that they name: `owner_list`: no device owns more than 2 matrices, and at least one owns 2. `stats`: Symmetric.
All inputs are finite; a program needn't handle non-finite values.
Results may differ from a plain program's by a relative error of at most 0.0077.
Values may be sent and summed in bfloat16 or wider, within the bound.
No kernel may reach another device: no remote copies, remote signals or barrier semaphores. Data moves between devices by JAX's collectives and lax.ppermute only.
A program may use at most 128 MiB of HBM per device.

v0:
```python
import jax
import jax.numpy as jnp
from jax import lax
from jax.sharding import PartitionSpec as P


def refine(iterate):
    for sweep in range(2):
        iter_b = iterate.astype(jnp.bfloat16)
        square = jnp.einsum(
            "cki,ckj->cij", iter_b, iter_b, preferred_element_type=jnp.float32
        ).astype(jnp.bfloat16)
        iterate = 1.5 * iterate - 0.5 * jnp.einsum(
            "cik,ckj->cij", iter_b, square, preferred_element_type=jnp.float32
        )
    return iterate


def local(gradients, moments, stats, bases, second, owner_list):
    matrices, piece_rows, piece_cols = gradients.shape
    capacity = stats.shape[0]
    owners = lax.axis_size("owner")
    tensors = lax.axis_size("tensor")
    devices = owners * tensors
    myself = lax.axis_index(("owner", "tensor"))
    matrix_ids = jnp.arange(matrices, dtype=jnp.int32)
    shared = owner_list[:, None] == owner_list[None, :]
    earlier = matrix_ids[:, None] < matrix_ids[None, :]
    position = jnp.sum((shared & earlier).astype(jnp.int32), axis=0)
    slot_id = owner_list * capacity + position
    targets = (
        jnp.arange(devices, dtype=jnp.int32)[None, :] * capacity
        + jnp.arange(capacity, dtype=jnp.int32)[:, None]
    )
    selector = (targets[:, :, None] == slot_id[None, None, :]).astype(jnp.bfloat16)
    new_moments = (0.9 * moments.astype(jnp.float32) + 0.1 * gradients.astype(jnp.float32)).astype(
        jnp.bfloat16
    )
    flat_grads = gradients.reshape(matrices, piece_rows * piece_cols)
    flat_moms = new_moments.reshape(matrices, piece_rows * piece_cols)
    send_grads = jnp.einsum(
        "cdn,nk->cdk", selector, flat_grads, preferred_element_type=jnp.float32
    ).astype(jnp.bfloat16)
    send_moms = jnp.einsum(
        "cdn,nk->cdk", selector, flat_moms, preferred_element_type=jnp.float32
    ).astype(jnp.bfloat16)
    got_grads, got_moms = (
        lax.all_to_all(
            send_grads.reshape(capacity, devices, piece_rows, piece_cols),
            ("owner", "tensor"),
            split_axis=1,
            concat_axis=1,
            tiled=True,
        ),
        lax.all_to_all(
            send_moms.reshape(capacity, devices, piece_rows, piece_cols),
            ("owner", "tensor"),
            split_axis=1,
            concat_axis=1,
            tiled=True,
        ),
    )

    def assemble(pieces):
        blocks = pieces.reshape(capacity, owners, tensors, piece_rows, piece_cols)
        return blocks.transpose(0, 1, 3, 2, 4).reshape(
            capacity, owners * piece_rows, tensors * piece_cols
        )

    grad_mats = assemble(got_grads)
    moment_mats = assemble(got_moms)
    full_rows = grad_mats.shape[1]
    full_cols = grad_mats.shape[2]
    gram = jnp.einsum("cri,crj->cij", grad_mats, grad_mats, preferred_element_type=jnp.float32)
    stat_next = 0.95 * stats + 0.05 / full_rows * gram
    basis_b = bases.astype(jnp.bfloat16)
    rotated = jnp.einsum("crk,ckj->crj", grad_mats, basis_b, preferred_element_type=jnp.float32)
    second_next = 0.95 * second.astype(jnp.float32) + 0.05 * rotated * rotated
    moment_rot = jnp.einsum(
        "crk,ckj->crj", moment_mats, basis_b, preferred_element_type=jnp.float32
    )
    scaled = (moment_rot / (jnp.sqrt(second_next) + 1e-06)).astype(jnp.bfloat16)
    step_mats = jnp.einsum(
        "crj,ckj->crk", scaled, basis_b, preferred_element_type=jnp.float32
    ).astype(jnp.bfloat16)
    step_pieces = step_mats.reshape(capacity, owners, piece_rows, tensors, piece_cols).transpose(
        0, 1, 3, 2, 4
    )
    returned = lax.all_to_all(
        step_pieces.reshape(capacity, devices, piece_rows, piece_cols),
        ("owner", "tensor"),
        split_axis=1,
        concat_axis=1,
        tiled=True,
    )
    returned = returned.reshape(capacity, devices, piece_rows * piece_cols)
    update = jnp.einsum(
        "cdn,cdk->nk", selector, returned, preferred_element_type=jnp.float32
    ).astype(jnp.bfloat16)
    update = update.reshape(matrices, piece_rows, piece_cols)
    power = jnp.einsum(
        "cij,cjk->cik",
        stat_next,
        bases,
        precision=lax.Precision.HIGHEST,
        preferred_element_type=jnp.float32,
    )
    iterate = power / (
        2.0 * jnp.sqrt(full_cols * jnp.mean(power * power, axis=(1, 2), keepdims=True) + 1e-06)
    )
    iterate = refine(iterate)
    my_slots = myself * capacity + jnp.arange(capacity, dtype=jnp.int32)
    filled = jnp.any(my_slots[:, None] == slot_id[None, :], axis=1).astype(jnp.float32)[
        :, None, None
    ]
    new_stats = stat_next * filled
    new_bases = iterate * filled
    new_second = (second_next * filled).astype(jnp.bfloat16)
    return (new_moments, update, new_stats, new_bases, new_second)


def solution(mesh):
    placed = (
        P(None, "owner", "tensor"),
        P(None, "owner", "tensor"),
        P(("owner", "tensor"), None, None),
        P(("owner", "tensor"), None, None),
        P(("owner", "tensor"), None, None),
        P(),
    )
    return jax.shard_map(
        local,
        mesh=mesh,
        in_specs=placed,
        out_specs=(
            P(None, "owner", "tensor"),
            P(None, "owner", "tensor"),
            P(("owner", "tensor"), None, None),
            P(("owner", "tensor"), None, None),
            P(("owner", "tensor"), None, None),
        ),
        check_vma=False,
    )
```

profile of v0, /device:TPU:1, one launch (start us, length us, event | category | flops | bytes accessed | tf_op | source)
XLA Modules:
  0.0 206.2 jit_solution(12441411162503713069)
XLA Ops:
  0.6 2.9 %add_convert_fusion = bf16[160,48,128]{2,1,0:T(8,128)(2,1)S(1)} fusion(bf16[160,48,128]{2,1,0:T(8,128)(2,1)} %param.6, bf16[160,48,128]{2,1,0:T(8,128)(2,1)} %param.7), kind=kLoop, calls=%fused_computation.8 | loop fusion | flops 5898240 | bytes 5898240 | tf_op jit(solution)/shard_map/convert_element_type | solution.py:36
  3.5 0.0 copy-start.1
  3.6 0.0 copy-start.2
  3.6 1.9 reshape.103
  5.5 0.0 copy-done.2
  5.5 0.1 convert_reduce_fusion
  5.6 2.6 %convolution_convert_fusion.1 = bf16[2,128,6144]{2,1,0:T(8,128)(2,1)S(1)} fusion(bf16[160,6144,1]{1,0,2:T(8,128)(2,1)} %reshape.103, s32[2,128]{1,0:T(2,128)S(1)} %iota_add_fusion, s32[160]{0:T(256)S(1)} %multiply_add_fusion.1), kind=kOutput, calls=%fused_computation.2 | convolution fusion | flops 504930304 | bytes 5113472 | tf_op jit(solution)/shard_map/cdn,nk->cdk/dot_general | solution.py:44
  8.2 0.0 copy-done.1
  8.2 0.7 copy.50
  9.0 2.2 %copy.33 = bf16[2,128,48,128]{3,2,0,1:T(8,128)(2,1)} copy(bf16[2,128,48,128]{3,2,1,0:T(8,128)(2,1)S(1)} %bitcast.42) | data formatting | bytes 6291456 | tf_op jit(solution)/shard_map/reshape | solution.py:56
  11.2 11.5 %all-to-all-start = ((bf16[2,128,48,128]{3,2,0,1:T(8,128)(2,1)}), bf16[2,128,48,128]{3,2,0,1:T(8,128)(2,1)S(1)}, u32[]{:S(2)}, u32[]{:S(2)}) async-start(bf16[2,128,48,128]{3,2,0,1:T(8,128)(2,1)} %copy.33), calls=%async_computation | async-start | bytes 6291456 | tf_op jit(solution)/shard_map/all_to_all | solution.py:55
  22.7 4.0 %reshape.104 = bf16[160,6144,1]{1,0,2:T(8,128)(2,1)} reshape(bf16[160,48,128]{2,1,0:T(8,128)(2,1)} %param.6) | data formatting | bytes 3932160 | tf_op jit(solution)/shard_map/reshape | solution.py:39
  26.6 2.6 %convolution_convert_fusion = bf16[2,128,6144]{2,1,0:T(8,128)(2,1)S(1)} fusion(bf16[160,6144,1]{1,0,2:T(8,128)(2,1)} %reshape.104, s32[2,128]{1,0:T(2,128)S(1)} %iota_add_fusion, s32[160]{0:T(256)S(1)} %multiply_add_fusion.1), kind=kOutput, calls=%fused_computation.1 | convolution fusion | flops 504930304 | bytes 5113472 | tf_op jit(solution)/shard_map/cdn,nk->cdk/dot_general | solution.py:41
  29.3 0.7 copy.51
  30.0 2.2 %copy.36 = bf16[2,128,48,128]{3,2,0,1:T(8,128)(2,1)} copy(bf16[2,128,48,128]{3,2,1,0:T(8,128)(2,1)S(1)} %bitcast.44) | data formatting | bytes 6291456 | tf_op jit(solution)/shard_map/reshape | solution.py:49
  32.2 32.1 %all-to-all-done = bf16[2,128,48,128]{3,2,0,1:T(8,128)(2,1)S(1)} async-done(((bf16[2,128,48,128]{3,2,0,1:T(8,128)(2,1)}), bf16[2,128,48,128]{3,2,0,1:T(8,128)(2,1)S(1)}, u32[]{:S(2)}, u32[]{:S(2)}) %all-to-all-start) | async-done | bytes 3145760 | tf_op jit(solution)/shard_map/all_to_all | solution.py:55
  64.4 4.8 %all-to-all-start.1 = ((bf16[2,128,48,128]{3,2,0,1:T(8,128)(2,1)}), bf16[2,128,48,128]{3,2,0,1:T(8,128)(2,1)}, u32[]{:S(2)}, u32[]{:S(2)}) async-start(bf16[2,128,48,128]{3,2,0,1:T(8,128)(2,1)} %copy.36), calls=%async_computation.1 | async-start | bytes 6291456 | tf_op jit(solution)/shard_map/all_to_all | solution.py:48
  69.2 0.2 compare_reduce_fusion
  69.4 3.3 %copy.35 = bf16[2,32,48,4,128]{4,3,2,1,0:T(4,128)(2,1)} copy(bf16[2,32,48,4,128]{4,2,0,3,1:T(8,128)(2,1)S(1)} %bitcast.39) | data formatting | bytes 6291456 | tf_op jit(solution)/shard_map/transpose | solution.py:66
  72.7 5.7 %reshape.94 = bf16[2,1536,512]{2,1,0:T(8,128)(2,1)} reshape(bf16[2,32,48,4,128]{4,3,2,1,0:T(4,128)(2,1)} %copy.35) | data formatting | bytes 6291456 | tf_op jit(solution)/shard_map/reshape | solution.py:66
  78.4 32.1 %all-to-all-done.1 = bf16[2,128,48,128]{3,2,0,1:T(8,128)(2,1)} async-done(((bf16[2,128,48,128]{3,2,0,1:T(8,128)(2,1)}), bf16[2,128,48,128]{3,2,0,1:T(8,128)(2,1)}, u32[]{:S(2)}, u32[]{:S(2)}) %all-to-all-start.1) | async-done | bytes 3145760 | tf_op jit(solution)/shard_map/all_to_all | solution.py:48
  110.5 5.2 %copy.58 = bf16[2,32,4,48,128]{4,2,3,1,0:T(4,128)(2,1)} copy(bf16[2,32,4,48,128]{4,3,0,2,1:T(8,128)(2,1)} %bitcast.3) | data formatting | bytes 6291456 | tf_op jit(solution)/shard_map/reshape | solution.py:65
  115.7 4.0 %reshape.98 = bf16[2,1536,512]{2,1,0:T(8,128)(2,1)S(1)} reshape(bf16[2,32,48,4,128]{4,3,2,1,0:T(4,128)(2,1)} %bitcast.45) | data formatting | bytes 6291456 | tf_op jit(solution)/shard_map/reshape | solution.py:66
  119.7 8.5 %multiply_convert_fusion = (bf16[2,1536,512]{2,1,0:T(8,128)(2,1)}, f32[2,1536,512]{2,1,0:T(8,128)}) fusion(bf16[2,1536,512]{2,1,0:T(8,128)(2,1)} %param.10, f32[2]{0:T(128)S(1)} %convert_element_type.67, bf16[2,1536,512]{2,1,0:T(8,128)(2,1)S(1)} %reshape.98, f32[2,512,512]{2,1,0:T(8,128)} %param.9), kind=kOutput, calls=%fused_computation.6 | convolution fusion | flops 1622147072 | bytes 17825800 | tf_op jit(solution)/shard_map/crk,ckj->crj/dot_general | solution.py:77
  128.2 12.4 %convolution_convert_fusion.2 = bf16[2,1536,512]{2,1,0:T(8,128)(2,1)} fusion(bf16[2,1536,512]{2,1,0:T(8,128)(2,1)} %reshape.94, f32[2,1536,512]{2,1,0:T(8,128)} %get-tuple-element.10, bf16[2,1536,512]{2,1,0:T(8,128)(2,1)} %param.10, f32[2,512,512]{2,1,0:T(8,128)} %param.9), kind=kOutput, calls=%fused_computation.9 | convolution fusion | flops 3236429824 | bytes 17825792 | tf_op jit(solution)/shard_map/crj,ckj->crk/dot_general | solution.py:83
  140.6 5.5 %reshape.99 = bf16[2,32,48,4,128]{4,3,2,1,0:T(4,128)(2,1)} reshape(bf16[2,1536,512]{2,1,0:T(8,128)(2,1)} %convolution_convert_fusion.2) | data formatting | bytes 6291456 | tf_op jit(solution)/shard_map/reshape | solution.py:86
  146.1 4.2 %copy.48 = bf16[2,32,48,4,128]{4,2,0,3,1:T(8,128)(2,1)} copy(bf16[2,32,48,4,128]{4,3,2,1,0:T(4,128)(2,1)} %reshape.99) | data formatting | bytes 6291456 | tf_op jit(solution)/shard_map/reshape | solution.py:90
  150.3 4.9 %all-to-all-start.2 = ((bf16[2,128,48,128]{3,2,0,1:T(8,128)(2,1)}), bf16[2,128,48,128]{3,2,0,1:T(8,128)(2,1)}, u32[]{:S(2)}, u32[]{:S(2)}) async-start(bf16[2,128,48,128]{3,2,0,1:T(8,128)(2,1)} %bitcast.40), calls=%async_computation.2 | async-start | bytes 6291456 | tf_op jit(solution)/shard_map/all_to_all | solution.py:89
  155.2 0.0 copy-start
  155.2 5.0 %broadcast_multiply_fusion = (f32[2,512,512]{2,1,0:T(8,128)}, f32[2,512,512]{2,1,0:T(8,128)S(1)}) fusion(f32[2]{0:T(128)S(1)} %convert_element_type.67, bf16[2,1536,512]{2,1,0:T(8,128)(2,1)S(1)} %reshape.98, f32[2,512,512]{2,1,0:T(8,128)} %param.8), kind=kOutput, calls=%fused_computation.23 | convolution fusion | flops 1612709888 | bytes 9437192 | tf_op jit(solution)/shard_map/cri,crj->cij/dot_general | solution.py:74
  160.2 0.0 copy-done
  160.2 3.7 %multiply_reduce_fusion = (f32[2]{0:T(128)S(1)}, f32[2,512,512]{2,1,0:T(8,128)S(1)}) fusion(f32[2,512,512]{2,1,0:T(8,128)S(1)} %get-tuple-element.6, f32[2,512,512]{2,1,0:T(8,128)S(1)} %copy-done), kind=kOutput, calls=%fused_computation.14 | convolution fusion | flops 3222274048 | bytes 6291464 | tf_op jit(solution)/shard_map/cij,cjk->cik/dot_general | solution.py:101
  163.9 2.8 %multiply_subtract_fusion = f32[2,512,512]{2,1,0:T(8,128)} fusion(f32[2,512,512]{2,1,0:T(8,128)S(1)} %get-tuple-element.8, f32[2]{0:T(128)S(1)} %sqrt_multiply_fusion), kind=kOutput, calls=%fused_computation.13 | convolution fusion | flops 1078460416 | bytes 4194312 | tf_op jit(solution)/shard_map/cik,ckj->cij/dot_general | solution.py:13
  166.7 6.3 %subtract_multiply_fusion = f32[2,512,512]{2,1,0:T(8,128)} fusion(f32[2,512,512]{2,1,0:T(8,128)} %multiply_subtract_fusion, f32[2]{0:T(128)S(1)} %convert_element_type.67), kind=kOutput, calls=%fused_computation.12 | convolution fusion | flops 1077411840 | bytes 4194312 | tf_op jit(solution)/shard_map/cik,ckj->cij/dot_general | solution.py:13
  173.1 23.4 %all-to-all-done.2 = bf16[2,128,48,128]{3,2,0,1:T(8,128)(2,1)} async-done(((bf16[2,128,48,128]{3,2,0,1:T(8,128)(2,1)}), bf16[2,128,48,128]{3,2,0,1:T(8,128)(2,1)}, u32[]{:S(2)}, u32[]{:S(2)}) %all-to-all-start.2) | async-done | bytes 3145760 | tf_op jit(solution)/shard_map/all_to_all | solution.py:89
  196.4 6.0 %reshape.108 = bf16[2,128,6144]{2,0,1:T(2,128)(2,1)S(1)} reshape(bf16[2,128,48,128]{3,2,0,1:T(8,128)(2,1)} %all-to-all-done.2) | data formatting | bytes 6291456 | tf_op jit(solution)/shard_map/reshape | solution.py:96
  202.4 2.1 %fusion.3 = bf16[20,8,48,128]{3,1,2,0:T(8,128)(2,1)S(1)} fusion(bf16[2,128,6144]{2,0,1:T(2,128)(2,1)S(1)} %reshape.108, s32[2,128]{1,0:T(2,128)S(1)} %iota_add_fusion, s32[160]{0:T(256)S(1)} %multiply_add_fusion.1), kind=kOutput, calls=%fused_computation.16 | convolution fusion | flops 504340480 | bytes 5113472 | tf_op jit(solution)/shard_map/cdn,cdk->nk/dot_general | solution.py:97
  204.5 1.7 copy.52
  (6 shorter events, 0.0 us)
Async XLA Ops:
  3.5 4.7 %copy-start.1 = (bf16[160,48,128]{2,1,0:T(8,128)(2,1)}, bf16[160,48,128]{2,1,0:T(8,128)(2,1)S(1)}, u32[]{:S(2)}) copy-start(bf16[160,48,128]{2,1,0:T(8,128)(2,1)S(1)} %add_convert_fusion) | copy-start | bytes 5898244
  3.6 1.9 copy-start.2
  11.2 53.2 %all-to-all-start = ((bf16[2,128,48,128]{3,2,0,1:T(8,128)(2,1)}), bf16[2,128,48,128]{3,2,0,1:T(8,128)(2,1)S(1)}, u32[]{:S(2)}, u32[]{:S(2)}) async-start(bf16[2,128,48,128]{3,2,0,1:T(8,128)(2,1)} %copy.33), calls=%async_computation | async-start | bytes 6291456 | tf_op jit(solution)/shard_map/all_to_all | solution.py:55
  64.4 46.2 %all-to-all-start.1 = ((bf16[2,128,48,128]{3,2,0,1:T(8,128)(2,1)}), bf16[2,128,48,128]{3,2,0,1:T(8,128)(2,1)}, u32[]{:S(2)}, u32[]{:S(2)}) async-start(bf16[2,128,48,128]{3,2,0,1:T(8,128)(2,1)} %copy.36), calls=%async_computation.1 | async-start | bytes 6291456 | tf_op jit(solution)/shard_map/all_to_all | solution.py:48
  150.3 46.1 %all-to-all-start.2 = ((bf16[2,128,48,128]{3,2,0,1:T(8,128)(2,1)}), bf16[2,128,48,128]{3,2,0,1:T(8,128)(2,1)}, u32[]{:S(2)}, u32[]{:S(2)}) async-start(bf16[2,128,48,128]{3,2,0,1:T(8,128)(2,1)} %bitcast.40), calls=%async_computation.2 | async-start | bytes 6291456 | tf_op jit(solution)/shard_map/all_to_all | solution.py:89
  155.2 5.0 %copy-start = (f32[2,512,512]{2,1,0:T(8,128)S(1)}, f32[2,512,512]{2,1,0:T(8,128)}, u32[]{:S(2)}) copy-start(f32[2,512,512]{2,1,0:T(8,128)} %param.9) | copy-start | bytes 6291460
where the time goes:
time: 207 us; the launch traced here: 206 us
  waiting for transfers between devices  87.6 us (42%)
  local copies, waits for them, and re-layouts  47.3 us (23%)
  matrix products  46.2 us (22%)
  starting transfers between devices  21.2 us (10%)
  other arithmetic  3.23 us (2%)
    all_to_all x1, waiting for transfers between devices, local(): lax.all_to_all(send_moms.reshape(capacity, devices, piece_rows, piece_col...  32.1 us
    all_to_all x1, waiting for transfers between devices, local(): lax.all_to_all(send_grads.reshape(capacity, devices, piece_rows, piece_co...  32.1 us
    all_to_all x1, waiting for transfers between devices, local(): lax.all_to_all(step_pieces.reshape(capacity, devices, piece_rows, piece_c...  23.4 us
    dot_general x1, matrix products, local(): jnp.einsum('crj,ckj->crk', scaled, basis_b, preferred_element_type=jnp.fl...  12.4 us
    all_to_all x1, starting transfers between devices, local(): lax.all_to_all(send_moms.reshape(capacity, devices, piece_rows, piece_col...  11.5 us
    reshape x2, local copies, waits for them, and re-layouts, assemble(): blocks.transpose(0, 1, 3, 2, 4)  9.76 us
    dot_general x2, matrix products, refine(): jnp.einsum('cik,ckj->cij', iter_b, square, preferred_element_type=jnp.flo...  9.13 us
    dot_general x1, matrix products, local(): jnp.einsum('crk,ckj->crj', grad_mats, basis_b, preferred_element_type=jnp...  8.48 us
  transfers between devices with their start and end apart: 3, of which 3 were waited for; matrix products, arithmetic and copies ran while one was open for 18% of the time, Pallas kernels for 0%

commit v1 on v0

--- a/solution.py
+++ b/solution.py
@@ -45,12 +45,20 @@
         "cdn,nk->cdk", selector, flat_moms, preferred_element_type=jnp.float32
     ).astype(jnp.bfloat16)
     got_grads, got_moms = (
-        lax.all_to_all(
-            send_grads.reshape(capacity, devices, piece_rows, piece_cols),
-            ("owner", "tensor"),
-            split_axis=1,
-            concat_axis=1,
-            tiled=True,
+        jnp.concatenate(
+            jax.lax.all_to_all(
+                jnp.stack(
+                    jnp.split(
+                        send_grads.reshape(capacity, devices, piece_rows, piece_cols),
+                        jax.lax.axis_size(("owner", "tensor")),
+                        1,
+                    )
+                ),
+                ("owner", "tensor"),
+                0,
+                0,
+            ),
+            1,
         ),
         lax.all_to_all(
             send_moms.reshape(capacity, devices, piece_rows, piece_cols),

time: 207 us -> 256 us (1.24)
  local copies, waits for them, and re-layouts: 47.3 us -> 123 us
  waiting for transfers between devices: 87.6 us -> 55.5 us
  starting transfers between devices: 21.2 us -> 26.5 us
    unnamed x9 -> x136, local copies, waits for them, and re-layouts: 3.15 us -> 80.1 us
    all_to_all x1, waiting for transfers between devices: 32.1 us -> 0.01 us  [local(): lax.all_to_all(send_moms.reshape(capacity, devices, piece_rows, piece_col...]
    reshape x2 -> x0, local copies, waits for them, and re-layouts: 7.38 us -> none  [the longest x1 5.17 us: assemble(): blocks = pieces.reshape(capacity, owners, tensors, piece_rows, piece_cols)]
    another operation x0 -> x2, local copies, waits for them, and re-layouts: none -> 5.77 us  [the longest x1 5.17 us: assemble(): blocks = pieces.reshape(capacity, owners, tensors, piece_rows, piece_cols)]
    all_to_all x1, starting transfers between devices: 4.85 us -> 10.2 us  [local(): jax.lax.all_to_all(jnp.stack(jnp.split(send_grads.reshape(capacity, devic...]
  transfers between devices with their start and end apart: 3 -> 3, of which waited for: 3 -> 2; matrix products, arithmetic and copies ran while one was open for 18% -> 44% of each run, Pallas kernels for 0% -> 0%
where the time goes in v1:
time: 256 us; the launch traced here: 255 us
  local copies, waits for them, and re-layouts  123 us (48%)
  waiting for transfers between devices  55.5 us (22%)
  matrix products  46.2 us (18%)
  starting transfers between devices  26.5 us (10%)
  other arithmetic  3.23 us (1%)
    unnamed x136, local copies, waits for them, and re-layouts  80.1 us
    all_to_all x1, waiting for transfers between devices, local(): jax.lax.all_to_all(jnp.stack(jnp.split(send_grads.reshape(capacity, devic...  32.1 us
    all_to_all x1, waiting for transfers between devices, local(): lax.all_to_all(step_pieces.reshape(capacity, devices, piece_rows, piece_c...  23.3 us
    dot_general x1, matrix products, local(): jnp.einsum('crj,ckj->crk', scaled, basis_b, preferred_element_type=jnp.fl...  12.4 us
    all_to_all x1, starting transfers between devices, local(): lax.all_to_all(send_moms.reshape(capacity, devices, piece_rows, piece_col...  11.5 us
    all_to_all x1, starting transfers between devices, local(): jax.lax.all_to_all(jnp.stack(jnp.split(send_grads.reshape(capacity, devic...  10.2 us
    reshape x2, local copies, waits for them, and re-layouts, assemble(): blocks.transpose(0, 1, 3, 2, 4)  9.76 us
    dot_general x2, matrix products, refine(): jnp.einsum('cik,ckj->cij', iter_b, square, preferred_element_type=jnp.flo...  9.13 us
  transfers between devices with their start and end apart: 3, of which 2 were waited for; matrix products, arithmetic and copies ran while one was open for 44% of the time, Pallas kernels for 0%

profile of v1, /device:TPU:1, one launch (start us, length us, event | category | flops | bytes accessed | tf_op | source)
XLA Modules:
  0.0 254.9 jit_solution(9153397402286933319)
XLA Ops:
  0.6 2.9 %add_convert_fusion = bf16[160,48,128]{2,1,0:T(8,128)(2,1)S(1)} fusion(bf16[160,48,128]{2,1,0:T(8,128)(2,1)} %param.6, bf16[160,48,128]{2,1,0:T(8,128)(2,1)} %param.7), kind=kLoop, calls=%fused_computation.8 | loop fusion | flops 5898240 | bytes 5898240 | tf_op jit(solution)/shard_map/convert_element_type | solution.py:36
  3.6 1.9 reshape.103
  5.6 2.6 %convolution_convert_fusion.1 = bf16[2,128,6144]{2,1,0:T(8,128)(2,1)S(1)} fusion(bf16[160,6144,1]{1,0,2:T(8,128)(2,1)} %reshape.103, s32[2,128]{1,0:T(2,128)S(1)} %iota_add_fusion, s32[160]{0:T(256)S(1)} %multiply_add_fusion.1), kind=kOutput, calls=%fused_computation.2 | convolution fusion | flops 504930304 | bytes 5113472 | tf_op jit(solution)/shard_map/cdn,nk->cdk/dot_general | solution.py:44
  8.2 0.7 copy.810
  9.0 2.2 copy.540
  11.2 11.5 %all-to-all-start = ((bf16[2,128,48,128]{3,2,0,1:T(8,128)(2,1)}), bf16[2,128,48,128]{3,2,0,1:T(8,128)(2,1)S(1)}, u32[]{:S(2)}, u32[]{:S(2)}) async-start(bf16[2,128,48,128]{3,2,0,1:T(8,128)(2,1)} %copy.540), calls=%async_computation | async-start | bytes 6291456 | tf_op jit(solution)/shard_map/all_to_all | solution.py:63
  22.7 4.0 %reshape.104 = bf16[160,6144,1]{1,0,2:T(8,128)(2,1)} reshape(bf16[160,48,128]{2,1,0:T(8,128)(2,1)} %param.6) | data formatting | bytes 3932160 | tf_op jit(solution)/shard_map/reshape | solution.py:39
  26.6 2.6 %convolution_convert_fusion = bf16[2,128,6144]{2,1,0:T(8,128)(2,1)S(1)} fusion(bf16[160,6144,1]{1,0,2:T(8,128)(2,1)} %reshape.104, s32[2,128]{1,0:T(2,128)S(1)} %iota_add_fusion, s32[160]{0:T(256)S(1)} %multiply_add_fusion.1), kind=kOutput, calls=%fused_computation.1 | convolution fusion | flops 504930304 | bytes 5113472 | tf_op jit(solution)/shard_map/cdn,nk->cdk/dot_general | solution.py:41
  29.3 0.7 copy.811
  30.6 0.6 constant_dynamic-update-slice_fusion.126
  33.6 0.6 constant_dynamic-update-slice_fusion.121
  36.1 0.6 constant_dynamic-update-slice_fusion.117
  38.5 0.6 constant_dynamic-update-slice_fusion.113
  40.9 0.6 constant_dynamic-update-slice_fusion.109
  42.7 0.6 constant_dynamic-update-slice_fusion.106
  43.3 0.6 constant_dynamic-update-slice_fusion.105
  45.1 0.6 constant_dynamic-update-slice_fusion.102
  50.0 0.6 constant_dynamic-update-slice_fusion.94
  54.8 0.6 constant_dynamic-update-slice_fusion.86
  57.2 0.6 constant_dynamic-update-slice_fusion.82
  57.8 0.6 constant_dynamic-update-slice_fusion.81
  62.1 0.6 constant_dynamic-update-slice_fusion.74
  62.7 0.6 constant_dynamic-update-slice_fusion.73
  64.5 0.6 constant_dynamic-update-slice_fusion.70
  67.5 0.6 constant_dynamic-update-slice_fusion.65
  70.0 0.6 constant_dynamic-update-slice_fusion.61
  74.2 0.6 constant_dynamic-update-slice_fusion.54
  74.8 0.6 constant_dynamic-update-slice_fusion.53
  77.2 0.6 constant_dynamic-update-slice_fusion.49
  79.1 0.6 constant_dynamic-update-slice_fusion.46
  79.7 0.6 constant_dynamic-update-slice_fusion.45
  81.5 0.6 constant_dynamic-update-slice_fusion.42
  84.5 0.6 constant_dynamic-update-slice_fusion.37
  87.5 0.6 constant_dynamic-update-slice_fusion.32
  89.4 0.6 constant_dynamic-update-slice_fusion.29
  91.2 0.6 constant_dynamic-update-slice_fusion.26
  91.8 0.6 constant_dynamic-update-slice_fusion.25
  93.6 0.6 constant_dynamic-update-slice_fusion.22
  94.3 0.6 constant_dynamic-update-slice_fusion.21
  96.1 0.6 constant_dynamic-update-slice_fusion.18
  98.5 0.6 constant_dynamic-update-slice_fusion.14
  99.1 0.6 constant_dynamic-update-slice_fusion.13
  100.9 0.6 constant_dynamic-update-slice_fusion.10
  104.0 0.6 constant_dynamic-update-slice_fusion.5
  106.4 0.6 constant_dynamic-update-slice_fusion.1
  107.6 10.2 %all-to-all-start.1 = ((bf16[128,2,1,48,128]{4,3,1,2,0:T(8,128)(2,1)}), bf16[128,2,1,48,128]{4,3,1,2,0:T(8,128)(2,1)}, u32[]{:S(2)}, u32[]{:S(2)}) async-start(bf16[128,2,1,48,128]{4,3,1,2,0:T(8,128)(2,1)} %constant_dynamic-update-slice_fusion), calls=%async_computation.1 | async-start | bytes 6291456 | tf_op jit(solution)/shard_map/all_to_all | solution.py:49
  118.0 3.3 %copy.542 = bf16[2,32,48,4,128]{4,3,2,1,0:T(4,128)(2,1)} copy(bf16[2,32,48,4,128]{4,2,0,3,1:T(8,128)(2,1)S(1)} %bitcast.935) | data formatting | bytes 6291456 | tf_op jit(solution)/shard_map/transpose | solution.py:74
  121.3 5.7 %reshape.94 = bf16[2,1536,512]{2,1,0:T(8,128)(2,1)} reshape(bf16[2,32,48,4,128]{4,3,2,1,0:T(4,128)(2,1)} %copy.542) | data formatting | bytes 6291456 | tf_op jit(solution)/shard_map/reshape | solution.py:74
  127.0 32.1 %all-to-all-done.1 = bf16[128,2,1,48,128]{4,3,1,2,0:T(8,128)(2,1)} async-done(((bf16[128,2,1,48,128]{4,3,1,2,0:T(8,128)(2,1)}), bf16[128,2,1,48,128]{4,3,1,2,0:T(8,128)(2,1)}, u32[]{:S(2)}, u32[]{:S(2)}) %all-to-all-start.1) | async-done | bytes 3145760 | tf_op jit(solution)/shard_map/all_to_all | solution.py:49
  159.2 5.2 %copy.818 = bf16[2,32,4,48,128]{4,2,3,1,0:T(4,128)(2,1)} copy(bf16[2,32,4,48,128]{4,3,0,2,1:T(8,128)(2,1)} %bitcast.132) | data formatting | bytes 6291456 | tf_op jit(solution)/shard_map/reshape;reshape | solution.py:73
  164.3 4.0 %reshape.98 = bf16[2,1536,512]{2,1,0:T(8,128)(2,1)S(1)} reshape(bf16[2,32,48,4,128]{4,3,2,1,0:T(4,128)(2,1)} %bitcast.940) | data formatting | bytes 6291456 | tf_op jit(solution)/shard_map/reshape | solution.py:74
  168.4 8.5 %multiply_convert_fusion = (bf16[2,1536,512]{2,1,0:T(8,128)(2,1)}, f32[2,1536,512]{2,1,0:T(8,128)}) fusion(bf16[2,1536,512]{2,1,0:T(8,128)(2,1)} %param.10, f32[2]{0:T(128)S(1)} %convert_element_type.67, bf16[2,1536,512]{2,1,0:T(8,128)(2,1)S(1)} %reshape.98, f32[2,512,512]{2,1,0:T(8,128)} %param.9), kind=kOutput, calls=%fused_computation.6 | convolution fusion | flops 1622147072 | bytes 17825800 | tf_op jit(solution)/shard_map/crk,ckj->crj/dot_general | solution.py:85
  176.9 12.4 %convolution_convert_fusion.2 = bf16[2,1536,512]{2,1,0:T(8,128)(2,1)} fusion(bf16[2,1536,512]{2,1,0:T(8,128)(2,1)} %reshape.94, f32[2,1536,512]{2,1,0:T(8,128)} %get-tuple-element.10, bf16[2,1536,512]{2,1,0:T(8,128)(2,1)} %param.10, f32[2,512,512]{2,1,0:T(8,128)} %param.9), kind=kOutput, calls=%fused_computation.9 | convolution fusion | flops 3236429824 | bytes 17825792 | tf_op jit(solution)/shard_map/crj,ckj->crk/dot_general | solution.py:91
  189.3 5.5 %reshape.99 = bf16[2,32,48,4,128]{4,3,2,1,0:T(4,128)(2,1)} reshape(bf16[2,1536,512]{2,1,0:T(8,128)(2,1)} %convolution_convert_fusion.2) | data formatting | bytes 6291456 | tf_op jit(solution)/shard_map/reshape | solution.py:94
  194.8 4.2 %copy.681 = bf16[2,32,48,4,128]{4,2,0,3,1:T(8,128)(2,1)} copy(bf16[2,32,48,4,128]{4,3,2,1,0:T(4,128)(2,1)} %reshape.99) | data formatting | bytes 6291456 | tf_op jit(solution)/shard_map/reshape | solution.py:98
  198.9 4.9 %all-to-all-start.2 = ((bf16[2,128,48,128]{3,2,0,1:T(8,128)(2,1)}), bf16[2,128,48,128]{3,2,0,1:T(8,128)(2,1)}, u32[]{:S(2)}, u32[]{:S(2)}) async-start(bf16[2,128,48,128]{3,2,0,1:T(8,128)(2,1)} %bitcast.936), calls=%async_computation.2 | async-start | bytes 6291456 | tf_op jit(solution)/shard_map/all_to_all | solution.py:97
  203.8 5.0 %broadcast_multiply_fusion = (f32[2,512,512]{2,1,0:T(8,128)}, f32[2,512,512]{2,1,0:T(8,128)S(1)}) fusion(f32[2]{0:T(128)S(1)} %convert_element_type.67, bf16[2,1536,512]{2,1,0:T(8,128)(2,1)S(1)} %reshape.98, f32[2,512,512]{2,1,0:T(8,128)} %param.8), kind=kOutput, calls=%fused_computation.23 | convolution fusion | flops 1612709888 | bytes 9437192 | tf_op jit(solution)/shard_map/cri,crj->cij/dot_general | solution.py:82
  208.9 3.7 %multiply_reduce_fusion = (f32[2]{0:T(128)S(1)}, f32[2,512,512]{2,1,0:T(8,128)S(1)}) fusion(f32[2,512,512]{2,1,0:T(8,128)S(1)} %get-tuple-element.6, f32[2,512,512]{2,1,0:T(8,128)S(1)} %copy-done), kind=kOutput, calls=%fused_computation.14 | convolution fusion | flops 3222274048 | bytes 6291464 | tf_op jit(solution)/shard_map/cij,cjk->cik/dot_general | solution.py:109
  212.6 2.8 %multiply_subtract_fusion = f32[2,512,512]{2,1,0:T(8,128)} fusion(f32[2,512,512]{2,1,0:T(8,128)S(1)} %get-tuple-element.8, f32[2]{0:T(128)S(1)} %sqrt_multiply_fusion), kind=kOutput, calls=%fused_computation.13 | convolution fusion | flops 1078460416 | bytes 4194312 | tf_op jit(solution)/shard_map/cik,ckj->cij/dot_general | solution.py:13
  215.4 6.3 %subtract_multiply_fusion = f32[2,512,512]{2,1,0:T(8,128)} fusion(f32[2,512,512]{2,1,0:T(8,128)} %multiply_subtract_fusion, f32[2]{0:T(128)S(1)} %convert_element_type.67), kind=kOutput, calls=%fused_computation.12 | convolution fusion | flops 1077411840 | bytes 4194312 | tf_op jit(solution)/shard_map/cik,ckj->cij/dot_general | solution.py:13
  221.7 23.3 %all-to-all-done.2 = bf16[2,128,48,128]{3,2,0,1:T(8,128)(2,1)} async-done(((bf16[2,128,48,128]{3,2,0,1:T(8,128)(2,1)}), bf16[2,128,48,128]{3,2,0,1:T(8,128)(2,1)}, u32[]{:S(2)}, u32[]{:S(2)}) %all-to-all-start.2) | async-done | bytes 3145760 | tf_op jit(solution)/shard_map/all_to_all | solution.py:97
  245.1 6.0 %reshape.108 = bf16[2,128,6144]{2,0,1:T(2,128)(2,1)S(1)} reshape(bf16[2,128,48,128]{3,2,0,1:T(8,128)(2,1)} %all-to-all-done.2) | data formatting | bytes 6291456 | tf_op jit(solution)/shard_map/reshape | solution.py:104
  251.1 2.1 fusion.3
  253.2 1.7 copy.812
  (107 shorter events, 55.7 us)
Async XLA Ops:
  3.5 4.7 %copy-start.1 = (bf16[160,48,128]{2,1,0:T(8,128)(2,1)}, bf16[160,48,128]{2,1,0:T(8,128)(2,1)S(1)}, u32[]{:S(2)}) copy-start(bf16[160,48,128]{2,1,0:T(8,128)(2,1)S(1)} %add_convert_fusion) | copy-start | bytes 5898244
  3.6 1.9 copy-start.2
  11.2 96.4 %all-to-all-start = ((bf16[2,128,48,128]{3,2,0,1:T(8,128)(2,1)}), bf16[2,128,48,128]{3,2,0,1:T(8,128)(2,1)S(1)}, u32[]{:S(2)}, u32[]{:S(2)}) async-start(bf16[2,128,48,128]{3,2,0,1:T(8,128)(2,1)} %copy.540), calls=%async_computation | async-start | bytes 6291456 | tf_op jit(solution)/shard_map/all_to_all | solution.py:63
  107.6 51.6 %all-to-all-start.1 = ((bf16[128,2,1,48,128]{4,3,1,2,0:T(8,128)(2,1)}), bf16[128,2,1,48,128]{4,3,1,2,0:T(8,128)(2,1)}, u32[]{:S(2)}, u32[]{:S(2)}) async-start(bf16[128,2,1,48,128]{4,3,1,2,0:T(8,128)(2,1)} %constant_dynamic-update-slice_fusion), calls=%async_computation.1 | async-start | bytes 6291456 | tf_op jit(solution)/shard_map/all_to_all | solution.py:49
  198.9 46.1 %all-to-all-start.2 = ((bf16[2,128,48,128]{3,2,0,1:T(8,128)(2,1)}), bf16[2,128,48,128]{3,2,0,1:T(8,128)(2,1)}, u32[]{:S(2)}, u32[]{:S(2)}) async-start(bf16[2,128,48,128]{3,2,0,1:T(8,128)(2,1)} %bitcast.936), calls=%async_computation.2 | async-start | bytes 6291456 | tf_op jit(solution)/shard_map/all_to_all | solution.py:97
  203.8 5.0 %copy-start = (f32[2,512,512]{2,1,0:T(8,128)S(1)}, f32[2,512,512]{2,1,0:T(8,128)}, u32[]{:S(2)}) copy-start(f32[2,512,512]{2,1,0:T(8,128)} %param.9) | copy-start | bytes 6291460
